TPU v7x, 128 devices: a whole 4x4x4 slice. The times are simulated.
128 devices in a mesh: layer: 16 (over y, x), prow: 4 (over z), pcol: 2 (over core).
Axes of the slice: x: 4, y: 4, z: 4, core: 2. Of those that a mesh axis runs over, the one named last changes fastest.
Arguments:
- front: bfloat16 [16, 2048, 32768], P('layer', 'prow', 'pcol'), may hold values from -6 to 6
- pivots: bfloat16 [16, 2, 256, 32768], P('layer', None, 'prow', 'pcol'), may hold values from -0.8984375 to 0.8984375
- inverses: bfloat16 [16, 2, 256, 256], P('layer'), may hold values from -0.1875 to 0.1875
- slab_pattern: int32 [16, 8, 128], P('layer', 'prow', 'pcol'), may hold values 0 or 1
- pivot_pattern: int32 [16, 2, 128], P('layer', None, 'pcol'), may hold values from 0 to 1, as said below
Outputs:
- ancestor: float32 [4, 16, 32, 32768], P('prow', 'layer', None, 'pcol')
- lower: bfloat16 [16, 2048, 512], P('layer', 'prow')
- upper: bfloat16 [16, 256, 32768], P('layer', 'prow', 'pcol')
Inputs may be any that keep to these rules, and one draw needn't show every extreme that they name: `pivot_pattern`: each entry says whether that block of the pivot rows is structurally nonzero. `slab_pattern`: each entry says whether that block of the front rows is structurally nonzero.
All inputs are finite; a program needn't handle non-finite values.
Results may differ from a plain program's by a relative error of at most 0.014.
Values may be sent and summed in bfloat16 or wider, within the bound.
No kernel may reach another device: no remote copies, remote signals or barrier semaphores. Data moves between devices by JAX's collectives and lax.ppermute only.
A program may use at most 192 MiB of HBM per device.

v0:
```python
import jax
import jax.numpy as jnp
from jax import lax
from jax.sharding import PartitionSpec as P


def spread(value, axis, root):
    mine = lax.axis_index(axis) == root
    return lax.psum(jnp.where(mine, value, jnp.zeros_like(value)), axis)


def on_device(front, pivots, inverses, slab_pattern, pivot_pattern):
    block_size = inverses.shape[-1]
    panel_width = 2 * block_size
    row_count = front.shape[1]
    col_count = front.shape[2]
    own_rows = pivots.shape[2]
    masked = (
        front[0].reshape(row_count // block_size, block_size, col_count // block_size, block_size)
        * slab_pattern[0].astype(jnp.bfloat16)[:, None, :, None]
    ).reshape(row_count, col_count)
    pivot_masked = (
        pivots[0].reshape(2, own_rows, col_count // block_size, block_size)
        * pivot_pattern[0].astype(jnp.bfloat16)[:, None, :, None]
    ).reshape(2, own_rows, col_count)
    first_inverse = inverses[0, 0]
    second_inverse = inverses[0, 1]
    row_offset = lax.axis_index("prow") * own_rows
    gathered = lax.all_gather(pivot_masked, "prow", axis=1, tiled=True)
    panel_cols = spread(
        jnp.concatenate(
            [masked[:, :panel_width], gathered[0][:, :panel_width], gathered[1][:, :panel_width]], 0
        ),
        "pcol",
        0,
    )
    front_cols = panel_cols[:row_count]
    pivot_cols = panel_cols[row_count : row_count + block_size]
    second_cols = panel_cols[row_count + block_size :]
    lower_pivot = jnp.dot(
        second_cols[:, :block_size], first_inverse, preferred_element_type=jnp.float32
    ).astype(jnp.bfloat16)
    upper_first = gathered[0]
    upper_second = (
        gathered[1].astype(jnp.float32)
        - jnp.dot(lower_pivot, upper_first, preferred_element_type=jnp.float32)
    ).astype(jnp.bfloat16)
    upper_own = lax.dynamic_slice_in_dim(upper_second, row_offset, own_rows, 0)
    lower_first = jnp.dot(
        front_cols[:, :block_size], first_inverse, preferred_element_type=jnp.float32
    ).astype(jnp.bfloat16)
    carried = (
        front_cols[:, block_size:].astype(jnp.float32)
        - jnp.dot(
            lower_first, pivot_cols[:, block_size:panel_width], preferred_element_type=jnp.float32
        )
    ).astype(jnp.bfloat16)
    lower_second = jnp.dot(carried, second_inverse, preferred_element_type=jnp.float32).astype(
        jnp.bfloat16
    )
    lower_panel = jnp.concatenate([lower_first, lower_second], 1)
    stacked = jnp.concatenate([upper_first, upper_second], 0)
    col_index = lax.axis_index("pcol") * col_count + jnp.arange(col_count, dtype=jnp.int32)
    retained = col_index >= panel_width
    schur_rows = masked.astype(jnp.float32) - jnp.dot(
        lower_panel, stacked, preferred_element_type=jnp.float32
    )
    schur_rows = jnp.where(retained[None, :], schur_rows, jnp.zeros_like(schur_rows))
    summed = lax.psum_scatter(
        schur_rows.astype(jnp.bfloat16), "layer", scatter_dimension=0, tiled=True
    ).astype(jnp.float32)
    ancestor = summed.reshape(1, 1, summed.shape[0], col_count)
    return (ancestor, lower_panel[None], upper_own[None])


def solution(mesh):
    placed = (
        P("layer", "prow", "pcol"),
        P("layer", None, "prow", "pcol"),
        P("layer", None, None, None),
        P("layer", "prow", "pcol"),
        P("layer", None, "pcol"),
    )
    return jax.shard_map(
        on_device,
        mesh=mesh,
        in_specs=placed,
        out_specs=(
            P("prow", "layer", None, "pcol"),
            P("layer", "prow", None),
            P("layer", "prow", "pcol"),
        ),
        check_vma=False,
    )
```

profile of v0, /device:TPU:1, one launch (start us, length us, event | category | flops | bytes accessed | tf_op | source)
XLA Modules:
  0.0 362.8 jit_solution(13036660158709411677)
XLA Ops:
  7.2 0.7 convert_bitcast_fusion
  7.9 0.1 broadcast_bitcast_fusion
  8.0 0.1 copy.10
  8.1 4.8 %bitcast_multiply_fusion.1 = bf16[2,64,16384]{2,1,0:T(8,128)(2,1)} fusion(bf16[1,2,64,16384]{3,2,1,0:T(8,128)(2,1)} %param.6, bf16[2,16384]{1,0:T(2,128)(2,1)S(1)} %bitcast.40), kind=kLoop, calls=%fused_computation.9 | loop fusion | flops 2097152 | bytes 8454144 | tf_op jit(solution)/shard_map/mul | solution.py:23
  12.9 0.0 all-reduce.2.cloned.1.call-start
  12.9 0.7 convert_bitcast_fusion.1
  13.6 2.7 mul.31
  16.3 10.4 %copy.9 = bf16[64,8,64,256]{3,1,2,0:T(8,128)(2,1)S(1)} copy(bf16[64,8,64,256]{3,2,1,0:T(8,128)(2,1)S(1)} %bitcast.39) | data formatting | bytes 33554432
  26.8 9.7 %bitcast_multiply_fusion = bf16[512,16384]{1,0:T(8,128)(2,1)S(1)} fusion(bf16[512,16384]{1,0:T(8,128)(2,1)S(1)} %bitcast.38, bf16[1,512,16384]{2,1,0:T(8,128)(2,1)} %param.5), kind=kLoop, calls=%fused_computation.6 | loop fusion | flops 8388608 | bytes 50331648 | tf_op jit(solution)/shard_map/mul | solution.py:19
  36.5 5.9 %copy-done = bf16[512,16384]{1,0:T(8,128)(2,1)} copy-done((bf16[512,16384]{1,0:T(8,128)(2,1)}, bf16[512,16384]{1,0:T(8,128)(2,1)S(1)}, u32[]{:S(2)}) %copy-start) | copy-done | bytes 16777240
  42.5 127.9 %all-gather.2.cloned.1.call-done = bf16[2,256,16384]{2,1,0:T(8,128)(2,1)} async-done(((bf16[2,64,16384]{2,1,0:T(8,128)(2,1)}), bf16[2,256,16384]{2,1,0:T(8,128)(2,1)}) %all-gather.2.cloned.1.call-update) | async-done | bytes 16777232 | tf_op jit(solution)/shard_map/all_gather | solution.py:29
  170.4 6.7 %slice_bitcast_fusion.1 = (bf16[256,16384]{1,0:T(8,128)(2,1)S(1)}, bf16[256,16384]{1,0:T(8,128)(2,1)S(1)}) fusion(bf16[2,256,16384]{2,1,0:T(8,128)(2,1)} %all-gather.2.cloned.1.call-done), kind=kLoop, calls=%fused_computation.8 | loop fusion | bytes 33554432 | tf_op jit(solution)/shard_map/squeeze | solution.py:32
  177.2 3.2 copy-done.1
  180.4 1.2 maximum_select_fusion
  181.6 0.0 reduce-scatter.2.cloned.1.call-start
  181.7 26.6 %all-reduce.2.cloned.1.call-done = bf16[1024,512]{1,0:T(8,128)(2,1)} async-done(((bf16[1024,512]{1,0:T(8,128)(2,1)}), bf16[1024,512]{1,0:T(8,128)(2,1)}) %all-reduce.2.cloned.1.call-update) | async-done | bytes 1048592 | tf_op jit(solution)/shard_map/psum | solution.py:9
  208.3 9.3 %fusion = bf16[256,16384]{1,0:T(8,128)(2,1)} fusion(bf16[1024,512]{1,0:T(8,128)(2,1)} %all-reduce.2.cloned.1.call-done, bf16[1,2,256,256]{3,2,1,0:T(8,128)(2,1)S(1)} %copy-done.2, bf16[2,256,16384]{2,1,0:T(8,128)(2,1)} %all-gather.2.cloned.1.call-done), kind=kOutput, calls=%fused_computation.2 | convolution fusion | flops 2193686528 | bytes 25427968 | tf_op jit(solution)/shard_map/dot_general | solution.py:46
  217.6 1.2 convolution_convert_fusion.1
  218.8 1.5 convolution_convert_fusion
  220.3 22.0 %select_convert_fusion = bf16[512,16384]{1,0:T(8,128)(2,1)} fusion(bf16[512,16384]{1,0:T(8,128)(2,1)} %copy-done, bf16[256,16384]{1,0:T(8,128)(2,1)} %fusion, bf16[256,16384]{1,0:T(8,128)(2,1)} %copy-done.1, pred[16384]{0:T(1024)(128)(4,1)S(1)} %add_compare_fusion, bf16[512,256]{0,1:T(8,128)(2,1)S(1)} %convolution_convert_fusion, ...), kind=kOutput, calls=%fused_computation | convolution fusion | flops 8658092032 | bytes 50872320 | tf_op jit(solution)/shard_map/dot_general | solution.py:65
  242.3 1.0 copy.8
  243.3 3.0 dynamic-slice_bitcast_fusion
  246.4 107.2 %reduce-scatter.2.cloned.1.call-done = bf16[32,16384]{1,0:T(8,128)(2,1)} async-done(((bf16[512,16384]{1,0:T(8,128)(2,1)}), bf16[32,16384]{1,0:T(8,128)(2,1)}) %reduce-scatter.2.cloned.1.call-update) | async-done | bytes 1048592 | tf_op jit(solution)/shard_map/reduce_scatter | solution.py:69
  353.6 2.7 bitcast_convert_fusion
  (13 shorter events, 0.2 us)
Async XLA Ops:
  7.2 163.2 %all-gather.2.cloned.1.call-start = ((), (), s32[]{:S(2)}) async-start(), calls=%async_computation.1 | async-start | bytes 20971520 | tf_op jit(solution)/shard_map/all_gather | solution.py:29
  12.9 195.4 %all-reduce.2.cloned.1.call-start = ((), (), s32[]{:S(2)}) async-start(), calls=%async_computation.2 | async-start | bytes 2097152 | tf_op jit(solution)/shard_map/psum | solution.py:9
  36.5 6.0 %copy-start = (bf16[512,16384]{1,0:T(8,128)(2,1)}, bf16[512,16384]{1,0:T(8,128)(2,1)S(1)}, u32[]{:S(2)}) copy-start(bf16[512,16384]{1,0:T(8,128)(2,1)S(1)} %bitcast_multiply_fusion) | copy-start | bytes 50331652
  42.5 165.8 %copy-start.2 = (bf16[1,2,256,256]{3,2,1,0:T(8,128)(2,1)S(1)}, bf16[1,2,256,256]{3,2,1,0:T(8,128)(2,1)}, u32[]{:S(2)}) copy-start(bf16[1,2,256,256]{3,2,1,0:T(8,128)(2,1)} %param.7) | copy-start | bytes 786436
  177.1 3.2 copy-start.1
  181.6 172.0 %reduce-scatter.2.cloned.1.call-start = ((), (), s32[]{:S(2)}) async-start(), calls=%async_computation.3 | async-start | bytes 17825792 | tf_op jit(solution)/shard_map/reduce_scatter | solution.py:69
Sparse Core Ops, SparseCore 0:
  13.0 157.3 all-gather.1
  181.7 26.5 all-reduce.1
  242.4 111.1 reduce-scatter.1
where the time goes:
time: 363 us
  waiting for transfers between devices  262 us (72%)
  matrix products  33.9 us (9%)
  local copies, waits for them, and re-layouts  33.3 us (9%)
  other arithmetic  19.8 us (5%)
  between operations  13.9 us (4%)
    all_gather x1, waiting for transfers between devices, on_device(): gathered = lax.all_gather(pivot_masked, 'prow', axis=1, tiled=True)  128 us
    reduce_scatter x1, waiting for transfers between devices, on_device(): lax.psum_scatter(schur_rows.astype(jnp.bfloat16), 'layer', scatter_dimens...  107 us
    psum x1, waiting for transfers between devices, spread(): return lax.psum(jnp.where(mine, value, jnp.zeros_like(value)), axis)  26.6 us
    dot_general x1, matrix products, on_device(): jnp.dot(lower_panel, stacked, preferred_element_type=jnp.float32)  22 us
    unnamed x10, local copies, waits for them, and re-layouts  20.7 us
    mul x1, other arithmetic, on_device(): front[0]  9.72 us
    dot_general x1, matrix products, on_device(): jnp.dot(lower_pivot, upper_first, preferred_element_type=jnp.float32)  9.25 us
  transfers between devices with their start and end apart: 3, of which 3 were waited for; matrix products, arithmetic and copies ran while one was open for 8% of the time, Pallas kernels for 0%

commit v1 on v0

--- a/solution.py
+++ b/solution.py
@@ -26,7 +26,8 @@
     first_inverse = inverses[0, 0]
     second_inverse = inverses[0, 1]
     row_offset = lax.axis_index("prow") * own_rows
-    gathered = lax.all_gather(pivot_masked, "prow", axis=1, tiled=True)
+    copies = jnp.concatenate([pivot_masked] * lax.axis_size("prow"), axis=1)
+    gathered = lax.all_to_all(copies, "prow", 1, 1, tiled=True)
     panel_cols = spread(
         jnp.concatenate(
             [masked[:, :panel_width], gathered[0][:, :panel_width], gathered[1][:, :panel_width]], 0

time: 363 us -> 475 us (1.31)
  local copies, waits for them, and re-layouts: 33.3 us -> 81.5 us
  waiting for transfers between devices: 262 us -> 290 us
  other arithmetic: 19.8 us -> 47.5 us
  starting transfers between devices: 0.12 us -> 7.59 us
    all_to_all x0 -> x1, waiting for transfers between devices: none -> 157 us  [on_device(): gathered = lax.all_to_all(copies, 'prow', 1, 1, tiled=True)]
    all_gather x1 -> x0, waiting for transfers between devices: 128 us -> none  [on_device(): gathered = lax.all_gather(pivot_masked, 'prow', axis=1, tiled=True)]
    slice x1 -> x2, local copies, waits for them, and re-layouts: 0.02 us -> 33.4 us  [on_device(): gathered[1][:, :panel_width]]
    concatenate x0 -> x1, other arithmetic: none -> 25.9 us  [on_device(): copies = jnp.concatenate([pivot_masked] * lax.axis_size('prow'), axis=1)]
    squeeze x1, local copies, waits for them, and re-layouts: 6.73 us -> 24 us  [on_device(): gathered[1][:, :panel_width]]
    all_to_all x0 -> x1, starting transfers between devices: none -> 7.1 us  [on_device(): gathered = lax.all_to_all(copies, 'prow', 1, 1, tiled=True)]
  transfers between devices with their start and end apart: 3 -> 3, of which waited for: 3 -> 3; matrix products, arithmetic and copies ran while one was open for 8% -> 5% of each run, Pallas kernels for 0% -> 0%
where the time goes in v1:
time: 475 us
  waiting for transfers between devices  290 us (61%)
  local copies, waits for them, and re-layouts  81.5 us (17%)
  other arithmetic  47.5 us (10%)
  matrix products  33.9 us (7%)
  between operations  14.2 us (3%)
  starting transfers between devices  7.59 us (2%)
    all_to_all x1, waiting for transfers between devices, on_device(): gathered = lax.all_to_all(copies, 'prow', 1, 1, tiled=True)  157 us
    reduce_scatter x1, waiting for transfers between devices, on_device(): lax.psum_scatter(schur_rows.astype(jnp.bfloat16), 'layer', scatter_dimens...  107 us
    slice x2, local copies, waits for them, and re-layouts, on_device(): gathered[1][:, :panel_width]  33.4 us
    concatenate x1, other arithmetic, on_device(): copies = jnp.concatenate([pivot_masked] * lax.axis_size('prow'), axis=1)  25.9 us
    psum x1, waiting for transfers between devices, spread(): return lax.psum(jnp.where(mine, value, jnp.zeros_like(value)), axis)  25.3 us
    squeeze x1, local copies, waits for them, and re-layouts, on_device(): gathered[1][:, :panel_width]  24 us
    dot_general x1, matrix products, on_device(): jnp.dot(lower_panel, stacked, preferred_element_type=jnp.float32)  22 us
    unnamed x10, local copies, waits for them, and re-layouts  17.3 us
  transfers between devices with their start and end apart: 3, of which 3 were waited for; matrix products, arithmetic and copies ran while one was open for 5% of the time, Pallas kernels for 0%

profile of v1, /device:TPU:1, one launch (start us, length us, event | category | flops | bytes accessed | tf_op | source)
XLA Modules:
  0.0 474.6 jit_solution(18373995428966968753)
XLA Ops:
  7.2 0.7 convert_bitcast_fusion
  8.0 8.7 %bitcast_multiply_fusion.1 = bf16[2,64,16384]{2,0,1:T(2,128)(2,1)S(1)} fusion(bf16[1,2,64,16384]{3,2,1,0:T(8,128)(2,1)} %param.6, bf16[2,16384]{1,0:T(2,128)(2,1)S(1)} %bitcast.38), kind=kLoop, calls=%fused_computation.10 | loop fusion | flops 2097152 | bytes 8454144 | tf_op jit(solution)/shard_map/mul | solution.py:23
  16.7 25.9 %pad_maximum_fusion = bf16[2,256,16384]{2,0,1:T(2,128)(2,1)} fusion(bf16[2,64,16384]{2,0,1:T(2,128)(2,1)S(1)} %bitcast_multiply_fusion.1), kind=kLoop, calls=%fused_computation.3 | loop fusion | flops 25165824 | bytes 20971520 | tf_op jit(solution)/shard_map/concatenate | solution.py:29
  42.7 7.1 %all-to-all-start = ((bf16[2,256,16384]{2,0,1:T(2,128)(2,1)}), bf16[2,256,16384]{2,0,1:T(2,128)(2,1)}, u32[]{:S(2)}, u32[]{:S(2)}) async-start(bf16[2,256,16384]{2,0,1:T(2,128)(2,1)} %pad_maximum_fusion), calls=%async_computation | async-start | bytes 33554432 | tf_op jit(solution)/shard_map/all_to_all | solution.py:30
  50.0 2.7 mul.31
  52.8 10.4 %copy.15 = bf16[64,8,64,256]{3,1,2,0:T(8,128)(2,1)S(1)} copy(bf16[64,8,64,256]{3,2,1,0:T(8,128)(2,1)S(1)} %bitcast.37) | data formatting | bytes 33554432
  63.2 8.3 %bitcast_multiply_fusion = bf16[512,16384]{1,0:T(8,128)(2,1)S(1)} fusion(bf16[512,16384]{1,0:T(8,128)(2,1)S(1)} %bitcast.36, bf16[1,512,16384]{2,1,0:T(8,128)(2,1)} %param.5), kind=kLoop, calls=%fused_computation.7 | loop fusion | flops 8388608 | bytes 50331648 | tf_op jit(solution)/shard_map/mul | solution.py:19
  71.5 5.7 %copy-done = bf16[512,16384]{1,0:T(8,128)(2,1)} copy-done((bf16[512,16384]{1,0:T(8,128)(2,1)}, bf16[512,16384]{1,0:T(8,128)(2,1)S(1)}, u32[]{:S(2)}) %copy-start) | copy-done | bytes 16777240
  77.3 157.4 %all-to-all-done = bf16[2,256,16384]{2,0,1:T(2,128)(2,1)} async-done(((bf16[2,256,16384]{2,0,1:T(2,128)(2,1)}), bf16[2,256,16384]{2,0,1:T(2,128)(2,1)}, u32[]{:S(2)}, u32[]{:S(2)}) %all-to-all-start) | async-done | bytes 16777248 | tf_op jit(solution)/shard_map/all_to_all | solution.py:30
  234.7 32.5 %fusion.22 = (bf16[1,256,16384]{2,0,1:T(2,128)(2,1)S(1)}, bf16[1,256,16384]{2,0,1:T(2,128)(2,1)}) fusion(bf16[2,256,16384]{2,0,1:T(2,128)(2,1)} %all-to-all-done), kind=kLoop, calls=%fused_computation.37 | loop fusion | bytes 33554432 | tf_op jit(solution)/shard_map/slice | solution.py:33
  267.2 24.0 %copy_bitcast_fusion = (bf16[256,16384]{1,0:T(8,128)(2,1)}, bf16[256,16384]{1,0:T(8,128)(2,1)}) fusion(bf16[1,256,16384]{2,0,1:T(2,128)(2,1)S(1)} %get-tuple-element.9, bf16[1,256,16384]{2,0,1:T(2,128)(2,1)} %get-tuple-element.10), kind=kLoop, calls=%fused_computation.8 | loop fusion | bytes 33554432 | tf_op jit(solution)/shard_map/squeeze | solution.py:33
  291.2 1.0 slice.55
  292.2 1.0 slice.57
  293.1 1.2 maximum_select_fusion
  294.3 0.3 reduce-scatter.2.cloned.1.call-start
  294.6 25.3 %all-reduce.2.cloned.1.call-done = bf16[1024,512]{1,0:T(8,128)(2,1)} async-done(((bf16[1024,512]{1,0:T(8,128)(2,1)}), bf16[1024,512]{1,0:T(8,128)(2,1)}) %all-reduce.2.cloned.1.call-update) | async-done | bytes 1048592 | tf_op jit(solution)/shard_map/psum | solution.py:9
  320.0 1.2 convolution_convert_fusion.1
  321.2 9.2 %fusion = bf16[256,16384]{1,0:T(8,128)(2,1)} fusion(bf16[256,16384]{1,0:T(8,128)(2,1)} %get-tuple-element.12, bf16[256,16384]{1,0:T(8,128)(2,1)} %get-tuple-element.11, bf16[1024,512]{1,0:T(8,128)(2,1)} %all-reduce.2.cloned.1.call-done, bf16[1,2,256,256]{3,2,1,0:T(8,128)(2,1)S(1)} %copy-done.1), kind=kOutput, calls=%fused_computation.2 | convolution fusion | flops 2193686528 | bytes 25427968 | tf_op jit(solution)/shard_map/dot_general | solution.py:47
  330.4 1.5 convolution_convert_fusion
  331.9 22.0 %select_convert_fusion = bf16[512,16384]{1,0:T(8,128)(2,1)} fusion(bf16[512,16384]{1,0:T(8,128)(2,1)} %copy-done, bf16[256,16384]{1,0:T(8,128)(2,1)} %fusion, bf16[256,16384]{1,0:T(8,128)(2,1)} %get-tuple-element.12, pred[16384]{0:T(1024)(128)(4,1)S(1)} %add_compare_fusion, bf16[512,256]{0,1:T(8,128)(2,1)S(1)} %convolution_convert_fusion, ...), kind=kOutput, calls=%fused_computation | convolution fusion | flops 8658092032 | bytes 50872320 | tf_op jit(solution)/shard_map/dot_general | solution.py:66
  353.9 1.0 copy.12
  354.9 3.0 dynamic-slice_bitcast_fusion
  358.0 107.1 %reduce-scatter.2.cloned.1.call-done = bf16[32,16384]{1,0:T(8,128)(2,1)} async-done(((bf16[512,16384]{1,0:T(8,128)(2,1)}), bf16[32,16384]{1,0:T(8,128)(2,1)}) %reduce-scatter.2.cloned.1.call-update) | async-done | bytes 1048592 | tf_op jit(solution)/shard_map/reduce_scatter | solution.py:70
  465.1 2.7 bitcast_convert_fusion
  (14 shorter events, 0.5 us)
Async XLA Ops:
  42.7 7.3 %copy-start.2 = (s32[1,2,64]{2,1,0:T(2,128)S(1)}, s32[1,2,64]{2,1,0:T(2,128)}, u32[]{:S(2)}) copy-start(s32[1,2,64]{2,1,0:T(2,128)} %param.8) | copy-start | bytes 1540
  42.7 192.1 %all-to-all-start = ((bf16[2,256,16384]{2,0,1:T(2,128)(2,1)}), bf16[2,256,16384]{2,0,1:T(2,128)(2,1)}, u32[]{:S(2)}, u32[]{:S(2)}) async-start(bf16[2,256,16384]{2,0,1:T(2,128)(2,1)} %pad_maximum_fusion), calls=%async_computation | async-start | bytes 33554432 | tf_op jit(solution)/shard_map/all_to_all | solution.py:30
  49.8 270.2 %all-reduce.2.cloned.1.call-start = ((), (), s32[]{:S(2)}) async-start(), calls=%async_computation.2 | async-start | bytes 2097152 | tf_op jit(solution)/shard_map/psum | solution.py:9
  71.5 5.7 %copy-start = (bf16[512,16384]{1,0:T(8,128)(2,1)}, bf16[512,16384]{1,0:T(8,128)(2,1)S(1)}, u32[]{:S(2)}) copy-start(bf16[512,16384]{1,0:T(8,128)(2,1)S(1)} %bitcast_multiply_fusion) | copy-start | bytes 50331652
  267.2 52.8 %copy-start.1 = (bf16[1,2,256,256]{3,2,1,0:T(8,128)(2,1)S(1)}, bf16[1,2,256,256]{3,2,1,0:T(8,128)(2,1)}, u32[]{:S(2)}) copy-start(bf16[1,2,256,256]{3,2,1,0:T(8,128)(2,1)} %param.7) | copy-start | bytes 786436
  294.3 170.7 %reduce-scatter.2.cloned.1.call-start = ((), (), s32[]{:S(2)}) async-start(), calls=%async_computation.3 | async-start | bytes 17825792 | tf_op jit(solution)/shard_map/reduce_scatter | solution.py:70
Sparse Core Ops, SparseCore 0:
  294.5 25.4 all-reduce.1
  354.0 111.0 reduce-scatter.1
